TPU v7x, 128 devices: a whole 4x4x4 slice. The times are simulated.
128 devices in a mesh: pipe: 4 (over x), dp: 8 (over z, y_lo), tensor: 4 (over y_hi, core).
Axes of the slice: x: 4, y: 4 (y_hi: 2, y_lo: 2; y = y_hi * 2 + y_lo), z: 4, core: 2. Of those that a mesh axis runs over, the one named last changes fastest.
Arguments:
- section_inputs: bfloat16 [4, 4096, 4096], P('pipe', ('dp', 'tensor')), may hold values from -36 to 36
- norm_gain: bfloat16 [4, 4096], P('pipe'), may hold values from 0.5 to 1.5
- query_weight: bfloat16 [4, 4096, 4096], P('pipe', None, 'tensor'), may hold values from -0.09375 to 0.09375
- key_weight: bfloat16 [4, 4096, 512], P('pipe', None, 'tensor'), may hold values from -0.09375 to 0.09375
- value_weight: bfloat16 [4, 4096, 512], P('pipe', None, 'tensor'), may hold values from -0.09375 to 0.09375
- output_weight: bfloat16 [4, 4096, 4096], P('pipe', 'tensor'), may hold values from -0.09375 to 0.09375
- upstream_grad: bfloat16 [4096, 4096], P(('dp', 'tensor')), may hold values from -6 to 6
- document_ids: int32 [8, 512], P('dp'), may hold values from 0 to 3, never falling along the last dimension, each value on 1 to 256 neighbouring positions
Outputs:
- input_grads: bfloat16 [4, 4096, 4096], P('pipe', ('dp', 'tensor'))
- query_grads: float32 [4, 4096, 4096], P('pipe', 'dp', 'tensor')
- key_grads: float32 [4, 4096, 512], P('pipe', 'dp', 'tensor')
- value_grads: float32 [4, 4096, 512], P('pipe', 'dp', 'tensor')
- output_grads: float32 [4, 4096, 4096], P('pipe', 'tensor', 'dp')
Inputs may be any that keep to these rules, and one draw needn't show every extreme that they name: `document_ids`: along each sequence the document numbers never fall; each of the 4 documents holds 1 to 256 tokens, one of them exactly 256.
All inputs are finite; a program needn't handle non-finite values.
Results may differ from a plain program's by a relative error of at most 0.03.
Values may be sent and summed in bfloat16 or wider, within the bound.
No kernel may reach another device: no remote copies, remote signals or barrier semaphores. Data moves between devices by JAX's collectives and lax.ppermute only.
A program may use at most 256 MiB of HBM per device.

v0:
```python
import math

import jax
import jax.numpy as jnp
from jax import lax
from jax.sharding import PartitionSpec as P

HD = 128


epsilon = 1e-05
rope_base = 500000.0


def shifted(shard, axis, by):
    devices = lax.axis_size(axis)
    pairs = [(i, i + by) for i in range(devices) if 0 <= i + by < devices]
    return lax.ppermute(shard, axis, pairs)


def position_tables(document_ids, head_dim):
    seq_len = document_ids.shape[1]
    index = jnp.arange(seq_len, dtype=jnp.int32)
    earlier = (document_ids[:, None, :] < document_ids[:, :, None]).astype(jnp.int32)
    position = index[None, :] - jnp.sum(earlier, axis=2)
    half = head_dim // 2
    expo = jnp.arange(half, dtype=jnp.float32) * (2.0 / head_dim)
    freq = jnp.exp(expo * -math.log(rope_base))
    angle = position.astype(jnp.float32)[:, :, None] * freq
    same = document_ids[:, :, None] == document_ids[:, None, :]
    causal = index[:, None] >= index[None, :]
    visible = jnp.logical_and(same, causal[None])
    return (jnp.cos(angle), jnp.sin(angle), visible)


def rotate(vector, rot_cos, rot_sin, direction):
    half = vector.shape[-1] // 2
    first = vector[..., :half]
    second = vector[..., half:]
    return jnp.concatenate(
        [
            first * rot_cos - direction * second * rot_sin,
            second * rot_cos + direction * first * rot_sin,
        ],
        axis=-1,
    )


def normalize(rows, gain):
    values = rows.astype(jnp.float32)
    inverse = lax.rsqrt(jnp.mean(values * values, axis=-1, keepdims=True) + epsilon)
    unit_rows = values * inverse
    normed = (unit_rows * gain.astype(jnp.float32)).astype(jnp.bfloat16)
    return (inverse, unit_rows, normed)


def attention_forward(query_rot, key_rot, value_low, visible):
    scale = 1.0 / math.sqrt(HD)
    scores = (
        jnp.einsum("bqngd,bknd->bngqk", query_rot, key_rot, preferred_element_type=jnp.float32)
        * scale
    )
    expo = jnp.where(visible[:, None, None], jnp.exp(scores), 0.0)
    prob = expo / jnp.sum(expo, axis=-1, keepdims=True)
    prob_low = prob.astype(jnp.bfloat16)
    mixed = jnp.einsum("bngqk,bknd->bqngd", prob_low, value_low, preferred_element_type=jnp.float32)
    return (prob, prob_low, mixed.astype(jnp.bfloat16))


def attention_backward(grad_mixed, query_rot, key_rot, value_low, prob, prob_low, rot_cos, rot_sin):
    scale = 1.0 / math.sqrt(HD)
    grad_value = jnp.einsum(
        "bngqk,bqngd->bknd", prob_low, grad_mixed, preferred_element_type=jnp.float32
    )
    grad_prob = jnp.einsum(
        "bqngd,bknd->bngqk", grad_mixed, value_low, preferred_element_type=jnp.float32
    )
    grad_score = prob * (grad_prob - jnp.sum(grad_prob * prob, axis=-1, keepdims=True)) * scale
    score_low = grad_score.astype(jnp.bfloat16)
    grad_query = jnp.einsum(
        "bngqk,bknd->bqngd", score_low, key_rot, preferred_element_type=jnp.float32
    )
    grad_key = jnp.einsum(
        "bngqk,bqngd->bknd", score_low, query_rot, preferred_element_type=jnp.float32
    )
    grad_query = rotate(
        grad_query, rot_cos[:, :, None, None, :], rot_sin[:, :, None, None, :], -1.0
    )
    grad_key = rotate(grad_key, rot_cos[:, :, None, :], rot_sin[:, :, None, :], -1.0)
    return (
        grad_query.astype(jnp.bfloat16),
        grad_key.astype(jnp.bfloat16),
        grad_value.astype(jnp.bfloat16),
    )


def back_norm(grad_normed, unit_rows, inverse, gain, incoming):
    grad_unit = grad_normed * gain.astype(jnp.float32)
    branch = (
        grad_unit - unit_rows * jnp.mean(grad_unit * unit_rows, axis=-1, keepdims=True)
    ) * inverse
    return (incoming.astype(jnp.float32) + branch).astype(jnp.bfloat16)


def local(
    section_inputs,
    norm_gain,
    query_weight,
    key_weight,
    value_weight,
    output_weight,
    upstream_grad,
    document_ids,
):
    pipes = lax.axis_size("pipe")
    section = lax.axis_index("pipe")
    groups = lax.axis_size("dp")
    width = section_inputs.shape[2]
    seq_len = document_ids.shape[1]
    q_width = query_weight.shape[2]
    k_width = key_weight.shape[2]
    kv_local = k_width // HD
    group = q_width // k_width
    gain = norm_gain[0]
    w_query = query_weight[0]
    w_key = key_weight[0]
    w_value = value_weight[0]
    w_output = output_weight[0]
    rot_cos, rot_sin, visible = position_tables(document_ids, HD)
    last = pipes - 1
    inverse, unit_rows, normed_shard = normalize(section_inputs[0], gain)
    normed = lax.all_gather(normed_shard, "tensor", axis=0, tiled=True)
    incoming = jnp.where(section == last, upstream_grad, jnp.zeros_like(upstream_grad))
    query = jnp.dot(normed, w_query, preferred_element_type=jnp.float32).reshape(
        1, seq_len, kv_local, group, HD
    )
    keys = jnp.dot(normed, w_key, preferred_element_type=jnp.float32).reshape(
        1, seq_len, kv_local, HD
    )
    values = jnp.dot(normed, w_value, preferred_element_type=jnp.float32).reshape(
        1, seq_len, kv_local, HD
    )
    query_rot = rotate(
        query, rot_cos[:, :, None, None, :], rot_sin[:, :, None, None, :], 1.0
    ).astype(jnp.bfloat16)
    key_rot = rotate(keys, rot_cos[:, :, None, :], rot_sin[:, :, None, :], 1.0).astype(jnp.bfloat16)
    value_low = values.astype(jnp.bfloat16)
    prob, prob_low, mixed = attention_forward(query_rot, key_rot, value_low, visible)
    mixed_flat = mixed.reshape(seq_len, q_width)

    def backward_turn(cotangent):
        grad_mixed = jnp.einsum(
            "sd,hd->sh", cotangent, w_output, preferred_element_type=jnp.float32
        )
        grad_mixed = grad_mixed.astype(jnp.bfloat16).reshape(1, seq_len, kv_local, group, HD)
        grad_query, grad_key, grad_value = attention_backward(
            grad_mixed, query_rot, key_rot, value_low, prob, prob_low, rot_cos, rot_sin
        )
        flat_query = grad_query.reshape(seq_len, q_width)
        flat_key = grad_key.reshape(seq_len, k_width)
        flat_value = grad_value.reshape(seq_len, k_width)
        grad_normed = (
            jnp.einsum("sh,dh->sd", flat_query, w_query, preferred_element_type=jnp.float32)
            + jnp.einsum("sh,dh->sd", flat_key, w_key, preferred_element_type=jnp.float32)
            + jnp.einsum("sh,dh->sd", flat_value, w_value, preferred_element_type=jnp.float32)
        )
        return (grad_normed.astype(jnp.bfloat16), flat_query, flat_key, flat_value)

    def skipped_turn(cotangent):
        return (
            jnp.zeros((seq_len, width), jnp.bfloat16),
            jnp.zeros((seq_len, q_width), jnp.bfloat16),
            jnp.zeros((seq_len, k_width), jnp.bfloat16),
            jnp.zeros((seq_len, k_width), jnp.bfloat16),
        )

    saved_query = jnp.zeros((seq_len, q_width), jnp.bfloat16)
    saved_key = jnp.zeros((seq_len, k_width), jnp.bfloat16)
    saved_value = jnp.zeros((seq_len, k_width), jnp.bfloat16)
    saved_cot = jnp.zeros((seq_len, width), jnp.bfloat16)
    saved_input = jnp.zeros_like(incoming)
    for turn in range(pipes):
        active = section == last - turn
        cotangent = lax.all_gather(incoming, "tensor", axis=0, tiled=True)
        grad_normed, flat_query, flat_key, flat_value = lax.cond(
            active, backward_turn, skipped_turn, cotangent
        )
        summed = lax.psum_scatter(grad_normed, "tensor", scatter_dimension=0, tiled=True).astype(
            jnp.float32
        )
        result = back_norm(summed, unit_rows, inverse, gain, incoming)
        saved_query = jnp.where(active, flat_query, saved_query)
        saved_key = jnp.where(active, flat_key, saved_key)
        saved_value = jnp.where(active, flat_value, saved_value)
        saved_cot = jnp.where(active, cotangent, saved_cot)
        saved_input = jnp.where(active, result, saved_input)
        if turn + 1 < pipes:
            incoming = shifted(result, "pipe", -1)
    scale_out = 1.0 / math.sqrt(groups * seq_len)
    terms = (
        jnp.einsum("sd,sh->dh", normed, saved_query, preferred_element_type=jnp.float32).astype(
            jnp.bfloat16
        ),
        jnp.einsum("sd,sh->dh", normed, saved_key, preferred_element_type=jnp.float32).astype(
            jnp.bfloat16
        ),
        jnp.einsum("sd,sh->dh", normed, saved_value, preferred_element_type=jnp.float32).astype(
            jnp.bfloat16
        ),
        jnp.einsum("sh,sd->hd", mixed_flat, saved_cot, preferred_element_type=jnp.float32).astype(
            jnp.bfloat16
        ),
    )
    sums = (
        lax.psum_scatter(terms[0], "dp", scatter_dimension=0, tiled=True).astype(jnp.float32),
        lax.psum_scatter(terms[1], "dp", scatter_dimension=0, tiled=True).astype(jnp.float32),
        lax.psum_scatter(terms[2], "dp", scatter_dimension=0, tiled=True).astype(jnp.float32),
        lax.psum_scatter(terms[3], "dp", scatter_dimension=1, tiled=True).astype(jnp.float32),
    )
    query_grads = (sums[0] * scale_out)[None]
    key_grads = (sums[1] * scale_out)[None]
    value_grads = (sums[2] * scale_out)[None]
    output_grads = (sums[3] * scale_out)[None]
    return (saved_input[None], query_grads, key_grads, value_grads, output_grads)


def solution(mesh):
    placed = (
        P("pipe", ("dp", "tensor"), None),
        P("pipe", None),
        P("pipe", None, "tensor"),
        P("pipe", None, "tensor"),
        P("pipe", None, "tensor"),
        P("pipe", "tensor", None),
        P(("dp", "tensor"), None),
        P("dp", None),
    )
    return jax.shard_map(
        local,
        mesh=mesh,
        in_specs=placed,
        out_specs=(
            P("pipe", ("dp", "tensor"), None),
            P("pipe", "dp", "tensor"),
            P("pipe", "dp", "tensor"),
            P("pipe", "dp", "tensor"),
            P("pipe", "tensor", "dp"),
        ),
        check_vma=False,
    )
```

profile of v0, /device:TPU:9, one launch (start us, length us, event | category | flops | bytes accessed | tf_op | source)
XLA Modules:
  0.0 1198.3 jit_solution(9367947700847733925)
XLA Ops:
  13.3 11.5 copy.92
  26.4 26.2 %all-gather.8.cloned.1.call-done = bf16[512,4096]{1,0:T(8,128)(2,1)} async-done(((bf16[128,4096]{1,0:T(8,128)(2,1)}), bf16[512,4096]{1,0:T(8,128)(2,1)}) %all-gather.8.cloned.1.call-update) | async-done | bytes 4194320 | tf_op jit(solution)/shard_map/all_gather | solution.py:132
  75.8 17.0 %all-gather.6.cloned.1.call-done = bf16[512,4096]{1,0:T(8,128)(2,1)} async-done(((bf16[128,4096]{1,0:T(8,128)(2,1)}), bf16[512,4096]{1,0:T(8,128)(2,1)}) %all-gather.6.cloned.1.call-update) | async-done | bytes 4194320 | tf_op jit(solution)/shard_map/all_gather | solution.py:184
  92.8 13.7 %conditional.4 = (bf16[512,4096]{1,0:T(8,128)(2,1)}, bf16[512,1024]{0,1:T(8,128)(2,1)}, bf16[512,128]{0,1:T(8,128)(2,1)}, bf16[512,128]{0,1:T(8,128)(2,1)}) conditional(s32[]{:T(128)} %convert_element_type.262, () %tuple.40, (bf16[512,4096]{1,0:T(8,128)(2,1)}, bf16[1024,4096]{1,0:T(8,128)(2,1)}, bf16[1,512,1,128]{3,1,2,0:T(8,128)(2,1)S(1)}, ...), branch_computations={%region_3.4_spmd, %region_4.6_spmd} | conditional | flops 11835437056 | bytes 200048896 | solution.py:185
  106.5 99.8 %reduce-scatter.9.cloned.1.call-done = bf16[128,4096]{1,0:T(8,128)(2,1)} async-done(((bf16[512,4096]{1,0:T(8,128)(2,1)}), bf16[128,4096]{1,0:T(8,128)(2,1)}) %reduce-scatter.9.cloned.1.call-update) | async-done | bytes 1048592 | tf_op jit(solution)/shard_map/reduce_scatter | solution.py:188
  212.4 24.6 %collective-permute-done = bf16[128,4096]{1,0:T(8,128)(2,1)} collective-permute-done((bf16[128,4096]{1,0:T(8,128)(2,1)S(1)}, bf16[128,4096]{1,0:T(8,128)(2,1)}, u32[]{:S(2)}, u32[]{:S(2)}) %collective-permute-start) | collective-permute-done | bytes 1048608 | tf_op jit(solution)/shard_map/ppermute | solution.py:18
  237.0 39.5 %all-gather.10.cloned.1.call-done = bf16[512,4096]{1,0:T(8,128)(2,1)} async-done(((bf16[128,4096]{1,0:T(8,128)(2,1)}), bf16[512,4096]{1,0:T(8,128)(2,1)}) %all-gather.10.cloned.1.call-update) | async-done | bytes 4194320 | tf_op jit(solution)/shard_map/all_gather | solution.py:184
  276.5 13.9 %conditional.5 = (bf16[512,4096]{1,0:T(8,128)(2,1)}, bf16[512,1024]{0,1:T(8,128)(2,1)}, bf16[512,128]{0,1:T(8,128)(2,1)}, bf16[512,128]{0,1:T(8,128)(2,1)}) conditional(s32[]{:T(128)} %convert_element_type.274, () %tuple.42, (bf16[512,4096]{1,0:T(8,128)(2,1)}, bf16[1024,4096]{1,0:T(8,128)(2,1)}, bf16[1,512,1,128]{3,1,2,0:T(8,128)(2,1)S(1)}, ...), branch_computations={%region_8.9_spmd, %region_9.11_spmd} | conditional | flops 11835437056 | bytes 204243232 | solution.py:185
  290.5 99.8 %reduce-scatter.11.cloned.1.call-done = bf16[128,4096]{1,0:T(8,128)(2,1)} async-done(((bf16[512,4096]{1,0:T(8,128)(2,1)}), bf16[128,4096]{1,0:T(8,128)(2,1)}) %reduce-scatter.11.cloned.1.call-update) | async-done | bytes 1048592 | tf_op jit(solution)/shard_map/reduce_scatter | solution.py:188
  396.7 24.6 %collective-permute-done.1 = bf16[128,4096]{1,0:T(8,128)(2,1)} collective-permute-done((bf16[128,4096]{1,0:T(8,128)(2,1)S(1)}, bf16[128,4096]{1,0:T(8,128)(2,1)}, u32[]{:S(2)}, u32[]{:S(2)}) %collective-permute-start.1) | collective-permute-done | bytes 1048608 | tf_op jit(solution)/shard_map/ppermute | solution.py:18
  421.4 39.4 %all-gather.12.cloned.1.call-done = bf16[512,4096]{1,0:T(8,128)(2,1)} async-done(((bf16[128,4096]{1,0:T(8,128)(2,1)}), bf16[512,4096]{1,0:T(8,128)(2,1)}) %all-gather.12.cloned.1.call-update) | async-done | bytes 4194320 | tf_op jit(solution)/shard_map/all_gather | solution.py:184
  460.8 13.7 %conditional.6 = (bf16[512,4096]{1,0:T(8,128)(2,1)}, bf16[512,1024]{0,1:T(8,128)(2,1)}, bf16[512,128]{0,1:T(8,128)(2,1)}, bf16[512,128]{0,1:T(8,128)(2,1)}) conditional(s32[]{:T(128)} %convert_element_type.278, () %tuple.44, (bf16[512,4096]{1,0:T(8,128)(2,1)}, bf16[1024,4096]{1,0:T(8,128)(2,1)}, bf16[1,512,1,128]{3,1,2,0:T(8,128)(2,1)S(1)}, ...), branch_computations={%region_13.14_spmd, %region_14.16_spmd} | conditional | flops 11835437056 | bytes 204243232 | solution.py:185
  474.5 98.5 %reduce-scatter.13.cloned.1.call-done = bf16[128,4096]{1,0:T(8,128)(2,1)} async-done(((bf16[512,4096]{1,0:T(8,128)(2,1)}), bf16[128,4096]{1,0:T(8,128)(2,1)}) %reduce-scatter.13.cloned.1.call-update) | async-done | bytes 1048592 | tf_op jit(solution)/shard_map/reduce_scatter | solution.py:188
  579.4 24.6 %collective-permute-done.2 = bf16[128,4096]{1,0:T(8,128)(2,1)} collective-permute-done((bf16[128,4096]{1,0:T(8,128)(2,1)S(1)}, bf16[128,4096]{1,0:T(8,128)(2,1)}, u32[]{:S(2)}, u32[]{:S(2)}) %collective-permute-start.2) | collective-permute-done | bytes 1048608 | tf_op jit(solution)/shard_map/ppermute | solution.py:18
  604.0 39.5 %all-gather.14.cloned.1.call-done = bf16[512,4096]{1,0:T(8,128)(2,1)} async-done(((bf16[128,4096]{1,0:T(8,128)(2,1)}), bf16[512,4096]{1,0:T(8,128)(2,1)}) %all-gather.14.cloned.1.call-update) | async-done | bytes 4194320 | tf_op jit(solution)/shard_map/all_gather | solution.py:184
  643.5 62.2 %conditional.7 = (bf16[512,4096]{1,0:T(8,128)(2,1)}, bf16[512,1024]{0,1:T(8,128)(2,1)}, bf16[512,128]{0,1:T(8,128)(2,1)}, bf16[512,128]{0,1:T(8,128)(2,1)}) conditional(s32[]{:T(128)} %convert_element_type.282, () %tuple.46, (bf16[512,4096]{1,0:T(8,128)(2,1)}, bf16[1024,4096]{1,0:T(8,128)(2,1)}, bf16[1,512,1,128]{3,1,2,0:T(8,128)(2,1)S(1)}, ...), branch_computations={%region_18.19_spmd, %region_19.21_spmd} | conditional | flops 11835437056 | bytes 204243232 | solution.py:185
  643.5 9.3 convolution_convert_fusion.3
  696.3 9.2 add_convert_fusion.6
  719.1 9.5 convolution_convert_fusion.4
  729.0 10.4 convolution_convert_fusion.5
  745.0 41.1 %reduce-scatter.19.cloned.1.call-done = bf16[512,128]{1,0:T(8,128)(2,1)} async-done(((bf16[4096,128]{1,0:T(8,128)(2,1)}), bf16[512,128]{1,0:T(8,128)(2,1)}) %reduce-scatter.19.cloned.1.call-update) | async-done | bytes 131088 | tf_op jit(solution)/shard_map/reduce_scatter | solution.py:216
  787.7 56.5 %reduce-scatter.15.cloned.1.call-done = bf16[128,4096]{1,0:T(8,128)(2,1)} async-done(((bf16[512,4096]{1,0:T(8,128)(2,1)}), bf16[128,4096]{1,0:T(8,128)(2,1)}) %reduce-scatter.15.cloned.1.call-update) | async-done | bytes 1048592 | tf_op jit(solution)/shard_map/reduce_scatter | solution.py:188
  849.7 166.4 %reduce-scatter.23.cloned.1.call-done = bf16[1024,512]{1,0:T(8,128)(2,1)} async-done(((bf16[1024,4096]{1,0:T(8,128)(2,1)}), bf16[1024,512]{1,0:T(8,128)(2,1)}) %reduce-scatter.23.cloned.1.call-update) | async-done | bytes 1048592 | tf_op jit(solution)/shard_map/reduce_scatter | solution.py:218
  1018.9 169.8 %reduce-scatter.17.cloned.1.call-done = bf16[512,1024]{1,0:T(8,128)(2,1)} async-done(((bf16[4096,1024]{1,0:T(8,128)(2,1)}), bf16[512,1024]{1,0:T(8,128)(2,1)}) %reduce-scatter.17.cloned.1.call-update) | async-done | bytes 1048592 | tf_op jit(solution)/shard_map/reduce_scatter | solution.py:215
  (139 shorter events, 139.9 us)
Async XLA Ops:
  7.2 45.4 %all-gather.8.cloned.1.call-start = ((), (), s32[]{:S(2)}) async-start(), calls=%async_computation.9 | async-start | bytes 5242880 | tf_op jit(solution)/shard_map/all_gather | solution.py:132
  12.1 80.6 %all-gather.6.cloned.1.call-start = ((), (), s32[]{:S(2)}) async-start(), calls=%async_computation.8 | async-start | bytes 5242880 | tf_op jit(solution)/shard_map/all_gather | solution.py:184
  13.3 193.1 %reduce-scatter.9.cloned.1.call-start = ((), (), s32[]{:S(2)}) async-start(), calls=%async_computation.10 | async-start | bytes 5242880 | tf_op jit(solution)/shard_map/reduce_scatter | solution.py:188
  13.3 11.5 copy-start.29
  13.3 39.3 %copy-start.2 = (bf16[1,4096,128]{2,1,0:T(8,128)(2,1)S(1)}, bf16[1,4096,128]{2,1,0:T(8,128)(2,1)}, u32[]{:S(2)}) copy-start(bf16[1,4096,128]{2,1,0:T(8,128)(2,1)} %param.19) | copy-start | bytes 3145732
  106.5 99.9 %copy-start = (bf16[1,128,4096]{2,1,0:T(8,128)(2,1)S(1)}, bf16[1,128,4096]{2,1,0:T(8,128)(2,1)}, u32[]{:S(2)}) copy-start(bf16[1,128,4096]{2,1,0:T(8,128)(2,1)} %param.16) | copy-start | bytes 3145732
  106.5 170.0 %all-gather.10.cloned.1.call-start = ((), (), s32[]{:S(2)}) async-start(), calls=%async_computation.11 | async-start | bytes 5242880 | tf_op jit(solution)/shard_map/all_gather | solution.py:184
  211.1 25.8 %collective-permute-start = (bf16[128,4096]{1,0:T(8,128)(2,1)S(1)}, bf16[128,4096]{1,0:T(8,128)(2,1)}, u32[]{:S(2)}, u32[]{:S(2)}) collective-permute-start(bf16[128,4096]{1,0:T(8,128)(2,1)S(1)} %fusion.104), channel_id=1, source_target_pairs={{32,0},{64,32},{96,64},{33,1},{65,33},{97,65},{34,2},{66,34},{98,6... | collective-permute-start | bytes 3145736 | tf_op jit(solution)/shard_map/ppermute | solution.py:18
  237.0 153.3 %reduce-scatter.11.cloned.1.call-start = ((), (), s32[]{:S(2)}) async-start(), calls=%async_computation.12 | async-start | bytes 5242880 | tf_op jit(solution)/shard_map/reduce_scatter | solution.py:188
  290.4 170.3 %all-gather.12.cloned.1.call-start = ((), (), s32[]{:S(2)}) async-start(), calls=%async_computation.13 | async-start | bytes 5242880 | tf_op jit(solution)/shard_map/all_gather | solution.py:184
  395.4 25.9 %collective-permute-start.1 = (bf16[128,4096]{1,0:T(8,128)(2,1)S(1)}, bf16[128,4096]{1,0:T(8,128)(2,1)}, u32[]{:S(2)}, u32[]{:S(2)}) collective-permute-start(bf16[128,4096]{1,0:T(8,128)(2,1)S(1)} %fusion.109), channel_id=1, source_target_pairs={{32,0},{64,32},{96,64},{33,1},{65,33},{97,65},{34,2},{66,34},{98,6... | collective-permute-start | bytes 3145736 | tf_op jit(solution)/shard_map/ppermute | solution.py:18
  421.3 151.7 %reduce-scatter.13.cloned.1.call-start = ((), (), s32[]{:S(2)}) async-start(), calls=%async_computation.14 | async-start | bytes 5242880 | tf_op jit(solution)/shard_map/reduce_scatter | solution.py:188
  474.5 169.0 %all-gather.14.cloned.1.call-start = ((), (), s32[]{:S(2)}) async-start(), calls=%async_computation.15 | async-start | bytes 5242880 | tf_op jit(solution)/shard_map/all_gather | solution.py:184
  578.1 25.8 %collective-permute-start.2 = (bf16[128,4096]{1,0:T(8,128)(2,1)S(1)}, bf16[128,4096]{1,0:T(8,128)(2,1)}, u32[]{:S(2)}, u32[]{:S(2)}) collective-permute-start(bf16[128,4096]{1,0:T(8,128)(2,1)S(1)} %fusion.114), channel_id=1, source_target_pairs={{32,0},{64,32},{96,64},{33,1},{65,33},{97,65},{34,2},{66,34},{98,6... | collective-permute-start | bytes 3145736 | tf_op jit(solution)/shard_map/ppermute | solution.py:18
  604.0 139.4 %reduce-scatter.21.cloned.1.call-start = ((), (), s32[]{:S(2)}) async-start(), calls=%async_computation.19 | async-start | bytes 1179648 | tf_op jit(solution)/shard_map/reduce_scatter | solution.py:217
  643.5 9.3 slice-start.6
  643.5 9.3 slice-start.7
  665.5 10.1 slice-start.14
  710.2 75.9 %reduce-scatter.19.cloned.1.call-start = ((), (), s32[]{:S(2)}) async-start(), calls=%async_computation.18 | async-start | bytes 1179648 | tf_op jit(solution)/shard_map/reduce_scatter | solution.py:216
  714.8 129.4 %reduce-scatter.15.cloned.1.call-start = ((), (), s32[]{:S(2)}) async-start(), calls=%async_computation.16 | async-start | bytes 5242880 | tf_op jit(solution)/shard_map/reduce_scatter | solution.py:188
  715.5 300.6 %reduce-scatter.23.cloned.1.call-start = ((), (), s32[]{:S(2)}) async-start(), calls=%async_computation.20 | async-start | bytes 9437184 | tf_op jit(solution)/shard_map/reduce_scatter | solution.py:218
  728.7 460.1 %reduce-scatter.17.cloned.1.call-start = ((), (), s32[]{:S(2)}) async-start(), calls=%async_computation.17 | async-start | bytes 9437184 | tf_op jit(solution)/shard_map/reduce_scatter | solution.py:215
  739.4 106.6 %copy-start.21 = (bf16[128,4096]{1,0:T(8,128)(2,1)S(1)}, bf16[128,4096]{1,0:T(8,128)(2,1)}, u32[]{:S(2)}) copy-start(bf16[128,4096]{1,0:T(8,128)(2,1)} %copy-done.20) | copy-start | bytes 3145732
  739.4 106.6 %copy-start.23 = (bf16[128,4096]{1,0:T(8,128)(2,1)S(1)}, bf16[128,4096]{1,0:T(8,128)(2,1)}, u32[]{:S(2)}) copy-start(bf16[128,4096]{1,0:T(8,128)(2,1)} %copy-done.22) | copy-start | bytes 3145732
  (13 other events, 50.7 us)
Sparse Core Ops, SparseCore 0:
  12.2 40.3 all-gather.7
  54.9 37.8 all-gather.5
  106.6 99.6 reduce-scatter.8
  237.1 39.3 all-gather.9
  290.6 99.6 reduce-scatter.10
  421.4 39.3 all-gather.11
  474.6 98.3 reduce-scatter.12
  604.1 39.3 all-gather.13
  710.3 32.9 reduce-scatter.20
  745.6 40.4 reduce-scatter.18
  788.7 55.4 reduce-scatter.14
  846.4 169.6 reduce-scatter.22
  1018.5 170.2 reduce-scatter.16
where the time goes:
time: 1210 us; the launch traced here: 1200 us
  waiting for transfers between devices  972 us (80%)
  matrix products  90.3 us (7%)
  other arithmetic  51.5 us (4%)
  local copies, waits for them, and re-layouts  38.6 us (3%)
  loops' own time  26.9 us (2%)
  between operations  14.4 us (1%)
    reduce_scatter x4, waiting for transfers between devices, local(): lax.psum_scatter(grad_normed, 'tensor', scatter_dimension=0, tiled=True)  355 us
    reduce_scatter x1, waiting for transfers between devices, local(): lax.psum_scatter(terms[0], 'dp', scatter_dimension=0, tiled=True)  170 us
    reduce_scatter x1, waiting for transfers between devices, local(): lax.psum_scatter(terms[3], 'dp', scatter_dimension=1, tiled=True)  166 us
    all_gather x4, waiting for transfers between devices, local(): cotangent = lax.all_gather(incoming, 'tensor', axis=0, tiled=True)  135 us
    ppermute x3, waiting for transfers between devices, shifted(): return lax.ppermute(shard, axis, pairs)  73.7 us
    reduce_scatter x1, waiting for transfers between devices, local(): lax.psum_scatter(terms[1], 'dp', scatter_dimension=0, tiled=True)  41.1 us
    another operation x14, local copies, waits for them, and re-layouts  34.1 us
    another operation x4, loops' own time, local(): lax.cond(active, backward_turn, skipped_turn, cotangent)  26.9 us
  transfers between devices with their start and end apart: 16, of which 16 were waited for; matrix products, arithmetic and copies ran while one was open for 6% of the time, Pallas kernels for 0%

commit v1 on v0

--- a/solution.py
+++ b/solution.py
@@ -16,6 +16,17 @@
     devices = lax.axis_size(axis)
     pairs = [(i, i + by) for i in range(devices) if 0 <= i + by < devices]
     return lax.ppermute(shard, axis, pairs)
+
+
+def exchange_sum(blocks, axis):
+    devices = lax.axis_size(axis)
+    me = lax.axis_index(axis)
+    total = lax.dynamic_index_in_dim(blocks, me, axis=0, keepdims=False).astype(jnp.float32)
+    for by in range(1, devices):
+        outgoing = lax.dynamic_index_in_dim(blocks, (me + by) % devices, axis=0, keepdims=False)
+        incoming = lax.ppermute(outgoing, axis, [(i, (i + by) % devices) for i in range(devices)])
+        total = total + incoming.astype(jnp.float32)
+    return total
 
 
 def position_tables(document_ids, head_dim):
@@ -185,9 +196,8 @@
         grad_normed, flat_query, flat_key, flat_value = lax.cond(
             active, backward_turn, skipped_turn, cotangent
         )
-        summed = lax.psum_scatter(grad_normed, "tensor", scatter_dimension=0, tiled=True).astype(
-            jnp.float32
-        )
+        tensors = lax.axis_size("tensor")
+        summed = exchange_sum(grad_normed.reshape(tensors, seq_len // tensors, width), "tensor")
         result = back_norm(summed, unit_rows, inverse, gain, incoming)
         saved_query = jnp.where(active, flat_query, saved_query)
         saved_key = jnp.where(active, flat_key, saved_key)
@@ -197,30 +207,23 @@
         if turn + 1 < pipes:
             incoming = shifted(result, "pipe", -1)
     scale_out = 1.0 / math.sqrt(groups * seq_len)
-    terms = (
-        jnp.einsum("sd,sh->dh", normed, saved_query, preferred_element_type=jnp.float32).astype(
-            jnp.bfloat16
-        ),
-        jnp.einsum("sd,sh->dh", normed, saved_key, preferred_element_type=jnp.float32).astype(
-            jnp.bfloat16
-        ),
-        jnp.einsum("sd,sh->dh", normed, saved_value, preferred_element_type=jnp.float32).astype(
-            jnp.bfloat16
-        ),
-        jnp.einsum("sh,sd->hd", mixed_flat, saved_cot, preferred_element_type=jnp.float32).astype(
-            jnp.bfloat16
-        ),
-    )
-    sums = (
-        lax.psum_scatter(terms[0], "dp", scatter_dimension=0, tiled=True).astype(jnp.float32),
-        lax.psum_scatter(terms[1], "dp", scatter_dimension=0, tiled=True).astype(jnp.float32),
-        lax.psum_scatter(terms[2], "dp", scatter_dimension=0, tiled=True).astype(jnp.float32),
-        lax.psum_scatter(terms[3], "dp", scatter_dimension=1, tiled=True).astype(jnp.float32),
-    )
-    query_grads = (sums[0] * scale_out)[None]
-    key_grads = (sums[1] * scale_out)[None]
-    value_grads = (sums[2] * scale_out)[None]
-    output_grads = (sums[3] * scale_out)[None]
+    grads_qkv = jnp.concatenate([saved_query, saved_key, saved_value], axis=1)
+    terms = jnp.concatenate(
+        [
+            jnp.einsum("sd,sh->dh", normed, grads_qkv, preferred_element_type=jnp.float32).astype(
+                jnp.bfloat16
+            ),
+            jnp.einsum("sd,sh->dh", saved_cot, mixed_flat, preferred_element_type=jnp.float32).astype(
+                jnp.bfloat16
+            ),
+        ],
+        axis=1,
+    )
+    sums = exchange_sum(terms.reshape(groups, width // groups, terms.shape[1]), "dp") * scale_out
+    query_grads = sums[:, :q_width][None]
+    key_grads = sums[:, q_width : q_width + k_width][None]
+    value_grads = sums[:, q_width + k_width : q_width + 2 * k_width][None]
+    output_grads = sums[:, q_width + 2 * k_width :].T[None]
     return (saved_input[None], query_grads, key_grads, value_grads, output_grads)
 
 

time: 1210 us -> 1150 us (0.950)
  waiting for transfers between devices: 972 us -> 833 us
  local copies, waits for them, and re-layouts: 38.6 us -> 91 us
  other arithmetic: 51.5 us -> 77.4 us
  starting transfers between devices: 4.58 us -> 30.1 us
  matrix products: 90.3 us -> 71.4 us
    reduce_scatter x8 -> x0, waiting for transfers between devices: 736 us -> none  [the longest x4 355 us: local(): lax.psum_scatter(grad_normed, 'tensor', scatter_dimension=0, tiled=True)]
    ppermute x0 -> x19, waiting for transfers between devices: none -> 461 us  [exchange_sum(): lax.ppermute(outgoing, axis, [(i, (i + by) % devices) for i in range(devi...]
    all_gather x4, waiting for transfers between devices: 135 us -> 229 us  [local(): cotangent = lax.all_gather(incoming, 'tensor', axis=0, tiled=True)]
    ppermute x3, waiting for transfers between devices: 73.7 us -> 118 us  [shifted(): return lax.ppermute(shard, axis, pairs)]
    reshape x0 -> x4, local copies, waits for them, and re-layouts: none -> 32.6 us  [the longest x1 24.8 us: local(): terms.reshape(groups, width // groups, terms.shape[1])]
    ppermute x0 -> x19, starting transfers between devices: none -> 26 us  [exchange_sum(): lax.ppermute(outgoing, axis, [(i, (i + by) % devices) for i in range(devi...]
    squeeze x0 -> x5, local copies, waits for them, and re-layouts: none -> 20.6 us  [exchange_sum(): lax.dynamic_index_in_dim(blocks, (me + by) % devices, axis=0, keepdims=Fa...]
    concatenate x0 -> x1, other arithmetic: none -> 17 us  [local(): jnp.concatenate([jnp.einsum('sd,sh->dh', normed, grads_qkv, preferred_ele...]
  transfers between devices with their start and end apart: 16 -> 27, of which waited for: 16 -> 23; matrix products, arithmetic and copies ran while one was open for 6% -> 4% of each run, Pallas kernels for 0% -> 0%
where the time goes in v1:
time: 1150 us; the launch traced here: 1140 us
  waiting for transfers between devices  833 us (72%)
  local copies, waits for them, and re-layouts  91 us (8%)
  other arithmetic  77.4 us (7%)
  matrix products  71.4 us (6%)
  starting transfers between devices  30.1 us (3%)
  loops' own time  19.3 us (2%)
  between operations  14.5 us (1%)
    ppermute x19, waiting for transfers between devices, exchange_sum(): lax.ppermute(outgoing, axis, [(i, (i + by) % devices) for i in range(devi...  461 us
    all_gather x4, waiting for transfers between devices, local(): cotangent = lax.all_gather(incoming, 'tensor', axis=0, tiled=True)  229 us
    ppermute x3, waiting for transfers between devices, shifted(): return lax.ppermute(shard, axis, pairs)  118 us
    another operation x11, local copies, waits for them, and re-layouts  26.9 us
    all_gather x1, waiting for transfers between devices, local(): normed = lax.all_gather(normed_shard, 'tensor', axis=0, tiled=True)  26.2 us
    ppermute x19, starting transfers between devices, exchange_sum(): lax.ppermute(outgoing, axis, [(i, (i + by) % devices) for i in range(devi...  26 us
    reshape x1, local copies, waits for them, and re-layouts, local(): terms.reshape(groups, width // groups, terms.shape[1])  24.8 us
  transfers between devices with their start and end apart: 27, of which 23 were waited for; matrix products, arithmetic and copies ran while one was open for 4% of the time, Pallas kernels for 0%

profile of v1, /device:TPU:9, one launch (start us, length us, event | category | flops | bytes accessed | tf_op | source)
XLA Modules:
  0.0 1137.2 jit_solution(15272532970423625581)
XLA Ops:
  13.4 11.4 %copy.116 = bf16[1024,4096]{1,0:T(8,128)(2,1)} copy(bf16[1024,4096]{0,1:T(8,128)(2,1)} %bitcast.671) | data formatting | bytes 16777216 | tf_op jit(solution)/shard_map/reshape.354
  26.4 26.2 %all-gather.8.cloned.1.call-done = bf16[512,4096]{1,0:T(8,128)(2,1)} async-done(((bf16[128,4096]{1,0:T(8,128)(2,1)}), bf16[512,4096]{1,0:T(8,128)(2,1)}) %all-gather.8.cloned.1.call-update) | async-done | bytes 4194320 | tf_op jit(solution)/shard_map/all_gather | solution.py:143
  75.7 17.1 %all-gather.6.cloned.1.call-done = bf16[512,4096]{1,0:T(8,128)(2,1)} async-done(((bf16[128,4096]{1,0:T(8,128)(2,1)}), bf16[512,4096]{1,0:T(8,128)(2,1)}) %all-gather.6.cloned.1.call-update) | async-done | bytes 4194320 | tf_op jit(solution)/shard_map/all_gather | solution.py:195
  110.6 19.0 %collective-permute-done = bf16[128,4096]{1,0:T(8,128)(2,1)} collective-permute-done((bf16[128,4096]{1,0:T(8,128)(2,1)}, bf16[128,4096]{1,0:T(8,128)(2,1)}, u32[]{:S(2)}, u32[]{:S(2)}) %collective-permute-start) | collective-permute-done | bytes 1048608 | tf_op jit(solution)/shard_map/ppermute | solution.py:27
  136.0 19.3 %collective-permute-done.1 = bf16[128,4096]{1,0:T(8,128)(2,1)} collective-permute-done((bf16[128,4096]{1,0:T(8,128)(2,1)}, bf16[128,4096]{1,0:T(8,128)(2,1)}, u32[]{:S(2)}, u32[]{:S(2)}) %collective-permute-start.1) | collective-permute-done | bytes 1048608 | tf_op jit(solution)/shard_map/ppermute | solution.py:27
  164.1 23.3 %collective-permute-done.3 = bf16[128,4096]{1,0:T(8,128)(2,1)} collective-permute-done((bf16[128,4096]{1,0:T(8,128)(2,1)S(1)}, bf16[128,4096]{1,0:T(8,128)(2,1)}, u32[]{:S(2)}, u32[]{:S(2)}) %collective-permute-start.3) | collective-permute-done | bytes 1048608 | tf_op jit(solution)/shard_map/ppermute | solution.py:18
  187.5 87.2 %all-gather.10.cloned.1.call-done = bf16[512,4096]{1,0:T(8,128)(2,1)} async-done(((bf16[128,4096]{1,0:T(8,128)(2,1)}), bf16[512,4096]{1,0:T(8,128)(2,1)}) %all-gather.10.cloned.1.call-update) | async-done | bytes 4194320 | tf_op jit(solution)/shard_map/all_gather | solution.py:195
  291.3 18.7 %collective-permute-done.4 = bf16[128,4096]{1,0:T(8,128)(2,1)S(1)} collective-permute-done((bf16[128,4096]{1,0:T(8,128)(2,1)S(1)}, bf16[128,4096]{1,0:T(8,128)(2,1)S(1)}, u32[]{:S(2)}, u32[]{:S(2)}) %collective-permute-start.4) | collective-permute-done | bytes 1048608 | tf_op jit(solution)/shard_map/ppermute | solution.py:27
  316.5 19.3 %collective-permute-done.5 = bf16[128,4096]{1,0:T(8,128)(2,1)S(1)} collective-permute-done((bf16[128,4096]{1,0:T(8,128)(2,1)S(1)}, bf16[128,4096]{1,0:T(8,128)(2,1)S(1)}, u32[]{:S(2)}, u32[]{:S(2)}) %collective-permute-start.5) | collective-permute-done | bytes 1048608 | tf_op jit(solution)/shard_map/ppermute | solution.py:27
  343.0 23.3 %collective-permute-done.7 = bf16[128,4096]{1,0:T(8,128)(2,1)} collective-permute-done((bf16[128,4096]{1,0:T(8,128)(2,1)S(1)}, bf16[128,4096]{1,0:T(8,128)(2,1)}, u32[]{:S(2)}, u32[]{:S(2)}) %collective-permute-start.7) | collective-permute-done | bytes 1048608 | tf_op jit(solution)/shard_map/ppermute | solution.py:18
  366.4 89.2 %all-gather.12.cloned.1.call-done = bf16[512,4096]{1,0:T(8,128)(2,1)} async-done(((bf16[128,4096]{1,0:T(8,128)(2,1)}), bf16[512,4096]{1,0:T(8,128)(2,1)}) %all-gather.12.cloned.1.call-update) | async-done | bytes 4194320 | tf_op jit(solution)/shard_map/all_gather | solution.py:195
  455.6 11.7 %conditional.6 = (bf16[512,1024]{0,1:T(8,128)(2,1)}, bf16[512,128]{0,1:T(8,128)(2,1)}, bf16[512,128]{0,1:T(8,128)(2,1)}, bf16[4,128,4096]{2,1,0:T(8,128)(2,1)}) conditional(s32[]{:T(128)} %convert_element_type.343, () %tuple.52, (bf16[512,4096]{1,0:T(8,128)(2,1)}, bf16[1024,4096]{1,0:T(8,128)(2,1)}, bf16[1,512,1,128]{3,1,2,0:T(8,128)(2,1)S(1)}, ...), branch_computations={%region_11.12_spmd, %region_12.14_spmd} | conditional | flops 11835437056 | bytes 154435776 | solution.py:196
  472.7 18.7 %collective-permute-done.8 = bf16[128,4096]{1,0:T(8,128)(2,1)S(1)} collective-permute-done((bf16[128,4096]{1,0:T(8,128)(2,1)S(1)}, bf16[128,4096]{1,0:T(8,128)(2,1)S(1)}, u32[]{:S(2)}, u32[]{:S(2)}) %collective-permute-start.8) | collective-permute-done | bytes 1048608 | tf_op jit(solution)/shard_map/ppermute | solution.py:27
  497.8 19.3 %collective-permute-done.9 = bf16[128,4096]{1,0:T(8,128)(2,1)S(1)} collective-permute-done((bf16[128,4096]{1,0:T(8,128)(2,1)S(1)}, bf16[128,4096]{1,0:T(8,128)(2,1)S(1)}, u32[]{:S(2)}, u32[]{:S(2)}) %collective-permute-start.9) | collective-permute-done | bytes 1048608 | tf_op jit(solution)/shard_map/ppermute | solution.py:27
  524.4 70.9 %collective-permute-done.11 = bf16[128,4096]{1,0:T(8,128)(2,1)} collective-permute-done((bf16[128,4096]{1,0:T(8,128)(2,1)S(1)}, bf16[128,4096]{1,0:T(8,128)(2,1)}, u32[]{:S(2)}, u32[]{:S(2)}) %collective-permute-start.11) | collective-permute-done | bytes 1048608 | tf_op jit(solution)/shard_map/ppermute | solution.py:18
  599.3 35.5 %all-gather.14.cloned.1.call-done = bf16[512,4096]{1,0:T(8,128)(2,1)} async-done(((bf16[128,4096]{1,0:T(8,128)(2,1)}), bf16[512,4096]{1,0:T(8,128)(2,1)}) %all-gather.14.cloned.1.call-update) | async-done | bytes 4194320 | tf_op jit(solution)/shard_map/all_gather | solution.py:195
  634.8 58.1 %conditional.7 = (bf16[512,1024]{0,1:T(8,128)(2,1)}, bf16[512,128]{0,1:T(8,128)(2,1)}, bf16[512,128]{0,1:T(8,128)(2,1)}, bf16[4,128,4096]{2,1,0:T(8,128)(2,1)}) conditional(s32[]{:T(128)} %convert_element_type.351, () %tuple.54, (bf16[512,4096]{1,0:T(8,128)(2,1)}, bf16[1024,4096]{1,0:T(8,128)(2,1)}, bf16[1,512,1,128]{3,1,2,0:T(8,128)(2,1)S(1)}, ...), branch_computations={%region_15.16_spmd, %region_16.18_spmd} | conditional | flops 11835437056 | bytes 179601664 | solution.py:196
  712.2 17.0 %pad_maximum_fusion.8 = bf16[4096,2304]{0,1:T(8,128)(2,1)} fusion(bf16[4096,1024]{0,1:T(8,128)(2,1)} %convolution_convert_fusion.5, bf16[4096,1280]{0,1:T(8,128)(2,1)S(1)} %convolution_convert_fusion.4), kind=kLoop, calls=%fused_computation.148 | loop fusion | flops 37748736 | bytes 37748736 | tf_op jit(solution)/shard_map/concatenate | solution.py:211
  729.1 24.8 %copy.118 = bf16[4096,2304]{1,0:T(8,128)(2,1)} copy(bf16[4096,2304]{0,1:T(8,128)(2,1)} %pad_maximum_fusion.8) | data formatting | bytes 37748736 | tf_op jit(solution)/shard_map/reshape | solution.py:222
  772.2 117.8 %collective-permute-done.12 = bf16[128,4096]{1,0:T(8,128)(2,1)} collective-permute-done((bf16[128,4096]{1,0:T(8,128)(2,1)S(1)}, bf16[128,4096]{1,0:T(8,128)(2,1)}, u32[]{:S(2)}, u32[]{:S(2)}) %collective-permute-start.12) | collective-permute-done | bytes 1048608 | tf_op jit(solution)/shard_map/ppermute | solution.py:27
  895.4 17.5 %collective-permute-done.13 = bf16[128,4096]{1,0:T(8,128)(2,1)} collective-permute-done((bf16[128,4096]{1,0:T(8,128)(2,1)S(1)}, bf16[128,4096]{1,0:T(8,128)(2,1)}, u32[]{:S(2)}, u32[]{:S(2)}) %collective-permute-start.13) | collective-permute-done | bytes 1048608 | tf_op jit(solution)/shard_map/ppermute | solution.py:27
  926.7 66.0 %collective-permute-done.20 = bf16[512,2304]{1,0:T(8,128)(2,1)} collective-permute-done((bf16[512,2304]{1,0:T(8,128)(2,1)}, bf16[512,2304]{1,0:T(8,128)(2,1)}, u32[]{:S(2)}, u32[]{:S(2)}) %collective-permute-start.20) | collective-permute-done | bytes 2359328 | tf_op jit(solution)/shard_map/ppermute | solution.py:27
  992.8 74.8 %collective-permute-done.18 = bf16[512,2304]{1,0:T(8,128)(2,1)} collective-permute-done((bf16[512,2304]{1,0:T(8,128)(2,1)}, bf16[512,2304]{1,0:T(8,128)(2,1)}, u32[]{:S(2)}, u32[]{:S(2)}) %collective-permute-start.18) | collective-permute-done | bytes 2359328 | tf_op jit(solution)/shard_map/ppermute | solution.py:27
  1067.5 50.5 %collective-permute-done.16 = bf16[512,2304]{1,0:T(8,128)(2,1)} collective-permute-done((bf16[512,2304]{1,0:T(8,128)(2,1)}, bf16[512,2304]{1,0:T(8,128)(2,1)}, u32[]{:S(2)}, u32[]{:S(2)}) %collective-permute-start.16) | collective-permute-done | bytes 2359328 | tf_op jit(solution)/shard_map/ppermute | solution.py:27
  (165 shorter events, 258.5 us)
Async XLA Ops:
  7.2 45.4 %all-gather.8.cloned.1.call-start = ((), (), s32[]{:S(2)}) async-start(), calls=%async_computation.1 | async-start | bytes 5242880 | tf_op jit(solution)/shard_map/all_gather | solution.py:143
  12.1 80.6 %all-gather.6.cloned.1.call-start = ((), (), s32[]{:S(2)}) async-start(), calls=%async_computation | async-start | bytes 5242880 | tf_op jit(solution)/shard_map/all_gather | solution.py:195
  13.3 261.5 %all-gather.10.cloned.1.call-start = ((), (), s32[]{:S(2)}) async-start(), calls=%async_computation.2 | async-start | bytes 5242880 | tf_op jit(solution)/shard_map/all_gather | solution.py:195
  108.8 27.3 %collective-permute-start.2 = (bf16[128,4096]{1,0:T(8,128)(2,1)}, bf16[128,4096]{1,0:T(8,128)(2,1)}, u32[]{:S(2)}, u32[]{:S(2)}) collective-permute-start(bf16[128,4096]{1,0:T(8,128)(2,1)} %get-tuple-element.386), channel_id=1, source_target_pairs={{0,3},{1,0},{2,1},{3,2},{4,7},{5,4},{6,5},{7,6},{8,11},{9,8},{10,9... | collective-permute-start | bytes 3145736 | tf_op jit(solution)/shard_map/ppermute | solution.py:27
  108.8 46.6 %collective-permute-start.1 = (bf16[128,4096]{1,0:T(8,128)(2,1)}, bf16[128,4096]{1,0:T(8,128)(2,1)}, u32[]{:S(2)}, u32[]{:S(2)}) collective-permute-start(bf16[128,4096]{1,0:T(8,128)(2,1)} %get-tuple-element.387), channel_id=1, source_target_pairs={{0,2},{1,3},{2,0},{3,1},{4,6},{5,7},{6,4},{7,5},{8,10},{9,11},{10,... | collective-permute-start | bytes 3145736 | tf_op jit(solution)/shard_map/ppermute | solution.py:27
  162.8 24.6 %collective-permute-start.3 = (bf16[128,4096]{1,0:T(8,128)(2,1)S(1)}, bf16[128,4096]{1,0:T(8,128)(2,1)}, u32[]{:S(2)}, u32[]{:S(2)}) collective-permute-start(bf16[128,4096]{1,0:T(8,128)(2,1)S(1)} %fusion.147), channel_id=1, source_target_pairs={{32,0},{64,32},{96,64},{33,1},{65,33},{97,65},{34,2},{66,34},{98,6... | collective-permute-start | bytes 3145736 | tf_op jit(solution)/shard_map/ppermute | solution.py:18
  187.5 268.1 %all-gather.12.cloned.1.call-start = ((), (), s32[]{:S(2)}) async-start(), calls=%async_computation.3 | async-start | bytes 5242880 | tf_op jit(solution)/shard_map/all_gather | solution.py:195
  289.5 27.0 %collective-permute-start.6 = (bf16[128,4096]{1,0:T(8,128)(2,1)S(1)}, bf16[128,4096]{1,0:T(8,128)(2,1)S(1)}, u32[]{:S(2)}, u32[]{:S(2)}) collective-permute-start(bf16[128,4096]{1,0:T(8,128)(2,1)S(1)} %get-tuple-element.383), channel_id=1, source_target_pairs={{0,3},{1,0},{2,1},{3,2},{4,7},{5,4},{6,5},{7,6},{8,11},{9,8},{10,9... | collective-permute-start | bytes 3145736 | tf_op jit(solution)/shard_map/ppermute | solution.py:27
  289.5 46.3 %collective-permute-start.5 = (bf16[128,4096]{1,0:T(8,128)(2,1)S(1)}, bf16[128,4096]{1,0:T(8,128)(2,1)S(1)}, u32[]{:S(2)}, u32[]{:S(2)}) collective-permute-start(bf16[128,4096]{1,0:T(8,128)(2,1)S(1)} %get-tuple-element.384), channel_id=1, source_target_pairs={{0,2},{1,3},{2,0},{3,1},{4,6},{5,7},{6,4},{7,5},{8,10},{9,11},{10,... | collective-permute-start | bytes 3145736 | tf_op jit(solution)/shard_map/ppermute | solution.py:27
  341.7 24.6 %collective-permute-start.7 = (bf16[128,4096]{1,0:T(8,128)(2,1)S(1)}, bf16[128,4096]{1,0:T(8,128)(2,1)}, u32[]{:S(2)}, u32[]{:S(2)}) collective-permute-start(bf16[128,4096]{1,0:T(8,128)(2,1)S(1)} %fusion.152), channel_id=1, source_target_pairs={{32,0},{64,32},{96,64},{33,1},{65,33},{97,65},{34,2},{66,34},{98,6... | collective-permute-start | bytes 3145736 | tf_op jit(solution)/shard_map/ppermute | solution.py:18
  366.3 268.5 %all-gather.14.cloned.1.call-start = ((), (), s32[]{:S(2)}) async-start(), calls=%async_computation.4 | async-start | bytes 5242880 | tf_op jit(solution)/shard_map/all_gather | solution.py:195
  470.9 27.0 %collective-permute-start.10 = (bf16[128,4096]{1,0:T(8,128)(2,1)S(1)}, bf16[128,4096]{1,0:T(8,128)(2,1)S(1)}, u32[]{:S(2)}, u32[]{:S(2)}) collective-permute-start(bf16[128,4096]{1,0:T(8,128)(2,1)S(1)} %get-tuple-element.380), channel_id=1, source_target_pairs={{0,3},{1,0},{2,1},{3,2},{4,7},{5,4},{6,5},{7,6},{8,11},{9,8},{10,9... | collective-permute-start | bytes 3145736 | tf_op jit(solution)/shard_map/ppermute | solution.py:27
  470.9 46.3 %collective-permute-start.9 = (bf16[128,4096]{1,0:T(8,128)(2,1)S(1)}, bf16[128,4096]{1,0:T(8,128)(2,1)S(1)}, u32[]{:S(2)}, u32[]{:S(2)}) collective-permute-start(bf16[128,4096]{1,0:T(8,128)(2,1)S(1)} %get-tuple-element.381), channel_id=1, source_target_pairs={{0,2},{1,3},{2,0},{3,1},{4,6},{5,7},{6,4},{7,5},{8,10},{9,11},{10,... | collective-permute-start | bytes 3145736 | tf_op jit(solution)/shard_map/ppermute | solution.py:27
  523.1 72.2 %collective-permute-start.11 = (bf16[128,4096]{1,0:T(8,128)(2,1)S(1)}, bf16[128,4096]{1,0:T(8,128)(2,1)}, u32[]{:S(2)}, u32[]{:S(2)}) collective-permute-start(bf16[128,4096]{1,0:T(8,128)(2,1)S(1)} %fusion.157), channel_id=1, source_target_pairs={{32,0},{64,32},{96,64},{33,1},{65,33},{97,65},{34,2},{66,34},{98,6... | collective-permute-start | bytes 3145736 | tf_op jit(solution)/shard_map/ppermute | solution.py:18
  764.4 151.1 %collective-permute-start.15 = (bf16[512,2304]{1,0:T(8,128)(2,1)S(1)}, bf16[512,2304]{1,0:T(8,128)(2,1)}, u32[]{:S(2)}, u32[]{:S(2)}) collective-permute-start(bf16[512,2304]{1,0:T(8,128)(2,1)S(1)} %get-tuple-element.365), channel_id=1, source_target_pairs={{0,4},{4,8},{8,12},{12,16},{16,20},{20,24},{24,28},{28,0},{1,5},{5... | collective-permute-start | bytes 7077896 | tf_op jit(solution)/shard_map/ppermute | solution.py:27
  766.6 150.4 %collective-permute-start.21 = (bf16[512,2304]{1,0:T(8,128)(2,1)S(1)}, bf16[512,2304]{1,0:T(8,128)(2,1)}, u32[]{:S(2)}, u32[]{:S(2)}) collective-permute-start(bf16[512,2304]{1,0:T(8,128)(2,1)S(1)} %get-tuple-element.366), channel_id=1, source_target_pairs={{0,28},{4,0},{8,4},{12,8},{16,12},{20,16},{24,20},{28,24},{1,29},{... | collective-permute-start | bytes 7077896 | tf_op jit(solution)/shard_map/ppermute | solution.py:27
  768.7 121.3 %collective-permute-start.12 = (bf16[128,4096]{1,0:T(8,128)(2,1)S(1)}, bf16[128,4096]{1,0:T(8,128)(2,1)}, u32[]{:S(2)}, u32[]{:S(2)}) collective-permute-start(bf16[128,4096]{1,0:T(8,128)(2,1)S(1)} %get-tuple-element.376), channel_id=1, source_target_pairs={{0,1},{1,2},{2,3},{3,0},{4,5},{5,6},{6,7},{7,4},{8,9},{9,10},{10,1... | collective-permute-start | bytes 3145736 | tf_op jit(solution)/shard_map/ppermute | solution.py:27
  769.9 121.7 %collective-permute-start.14 = (bf16[128,4096]{1,0:T(8,128)(2,1)S(1)}, bf16[128,4096]{1,0:T(8,128)(2,1)}, u32[]{:S(2)}, u32[]{:S(2)}) collective-permute-start(bf16[128,4096]{1,0:T(8,128)(2,1)S(1)} %get-tuple-element.377), channel_id=1, source_target_pairs={{0,3},{1,0},{2,1},{3,2},{4,7},{5,4},{6,5},{7,6},{8,11},{9,8},{10,9... | collective-permute-start | bytes 3145736 | tf_op jit(solution)/shard_map/ppermute | solution.py:27
  769.9 143.0 %collective-permute-start.13 = (bf16[128,4096]{1,0:T(8,128)(2,1)S(1)}, bf16[128,4096]{1,0:T(8,128)(2,1)}, u32[]{:S(2)}, u32[]{:S(2)}) collective-permute-start(bf16[128,4096]{1,0:T(8,128)(2,1)S(1)} %get-tuple-element.378), channel_id=1, source_target_pairs={{0,2},{1,3},{2,0},{3,1},{4,6},{5,7},{6,4},{7,5},{8,10},{9,11},{10,... | collective-permute-start | bytes 3145736 | tf_op jit(solution)/shard_map/ppermute | solution.py:27
  890.0 102.8 %collective-permute-start.20 = (bf16[512,2304]{1,0:T(8,128)(2,1)}, bf16[512,2304]{1,0:T(8,128)(2,1)}, u32[]{:S(2)}, u32[]{:S(2)}) collective-permute-start(bf16[512,2304]{1,0:T(8,128)(2,1)} %get-tuple-element.367), channel_id=1, source_target_pairs={{0,24},{4,28},{8,0},{12,4},{16,8},{20,12},{24,16},{28,20},{1,25},{... | collective-permute-start | bytes 7077896 | tf_op jit(solution)/shard_map/ppermute | solution.py:27
  891.6 101.2 %collective-permute-start.19 = (bf16[512,2304]{1,0:T(8,128)(2,1)}, bf16[512,2304]{1,0:T(8,128)(2,1)}, u32[]{:S(2)}, u32[]{:S(2)}) collective-permute-start(bf16[512,2304]{1,0:T(8,128)(2,1)} %get-tuple-element.368), channel_id=1, source_target_pairs={{0,20},{4,24},{8,28},{12,0},{16,4},{20,8},{24,12},{28,16},{1,21},{... | collective-permute-start | bytes 7077896 | tf_op jit(solution)/shard_map/ppermute | solution.py:27
  912.9 154.6 %collective-permute-start.18 = (bf16[512,2304]{1,0:T(8,128)(2,1)}, bf16[512,2304]{1,0:T(8,128)(2,1)}, u32[]{:S(2)}, u32[]{:S(2)}) collective-permute-start(bf16[512,2304]{1,0:T(8,128)(2,1)} %get-tuple-element.369), channel_id=1, source_target_pairs={{0,16},{4,20},{8,24},{12,28},{16,0},{20,4},{24,8},{28,12},{1,17},{... | collective-permute-start | bytes 7077896 | tf_op jit(solution)/shard_map/ppermute | solution.py:27
  915.5 152.1 %collective-permute-start.17 = (bf16[512,2304]{1,0:T(8,128)(2,1)}, bf16[512,2304]{1,0:T(8,128)(2,1)}, u32[]{:S(2)}, u32[]{:S(2)}) collective-permute-start(bf16[512,2304]{1,0:T(8,128)(2,1)} %get-tuple-element.370), channel_id=1, source_target_pairs={{0,12},{4,16},{8,20},{12,24},{16,28},{20,0},{24,4},{28,8},{1,13},{... | collective-permute-start | bytes 7077896 | tf_op jit(solution)/shard_map/ppermute | solution.py:27
  917.0 201.0 %collective-permute-start.16 = (bf16[512,2304]{1,0:T(8,128)(2,1)}, bf16[512,2304]{1,0:T(8,128)(2,1)}, u32[]{:S(2)}, u32[]{:S(2)}) collective-permute-start(bf16[512,2304]{1,0:T(8,128)(2,1)} %get-tuple-element.371), channel_id=1, source_target_pairs={{0,8},{4,12},{8,16},{12,20},{16,24},{20,28},{24,0},{28,4},{1,9},{5... | collective-permute-start | bytes 7077896 | tf_op jit(solution)/shard_map/ppermute | solution.py:27
  (27 other events, 1191.9 us)
Sparse Core Ops, SparseCore 0:
  12.2 40.3 all-gather.7
  54.8 37.8 all-gather.5
  187.6 87.0 all-gather.9
  366.4 89.1 all-gather.11
  595.4 39.3 all-gather.13
